TPU v7x, 32 devices: a whole 2x2x4 slice. The times are simulated.
32 devices in a mesh: dp: 4 (over z), expert: 8 (over y, x, core).
Axes of the slice: x: 2, y: 2, z: 4, core: 2. Of those that a mesh axis runs over, the one named last changes fastest.
Arguments:
- tokens: bfloat16 [384, 4096], P('expert', 'dp'), may hold values from -6 to 6
- out_grad: bfloat16 [384, 4096], P('expert', 'dp'), may hold values from -6 to 6
- expert_ids: int32 [384, 8], P('expert'), may hold values from 0 to 63, all different within a row; in each aligned block of 48 rows (0 to 47, 48 to 95, ...) at most 12 rows name the same one
- route_weights: float32 [384, 8], P('expert'), may hold values from 0.05 to 1
- gate_weight: bfloat16 [64, 4096, 768], P('expert', 'dp'), may hold values from -0.09375 to 0.09375
- up_weight: bfloat16 [64, 4096, 768], P('expert', 'dp'), may hold values from -0.09375 to 0.09375
- down_weight: bfloat16 [64, 768, 4096], P('expert', None, 'dp'), may hold values from -0.21875 to 0.21875
Outputs:
- layer_out: bfloat16 [384, 4096], P('expert', 'dp')
- grad_tokens: bfloat16 [384, 4096], P('expert', 'dp')
- gate_grad: bfloat16 [64, 4096, 768], P('expert', 'dp')
- up_grad: bfloat16 [64, 4096, 768], P('expert', 'dp')
- down_grad: bfloat16 [64, 768, 4096], P('expert', None, 'dp')
Inputs may be any that keep to these rules, and one draw needn't show every extreme that they name: `expert_ids`: each row names 8 different experts. In the 48 rows of one index of the expert axis no expert is named more than 12 times, and in every draw some expert is named exactly 12 times there.
All inputs are finite; a program needn't handle non-finite values.
Results may differ from a plain program's by a relative error of at most 0.029.
Values may be sent and summed in bfloat16 or wider, within the bound.
No kernel may reach another device: no remote copies, remote signals or barrier semaphores. Data moves between devices by JAX's collectives and lax.ppermute only.
A program may use at most 128 MiB of HBM per device.

v0:
```python
import jax
import jax.numpy as jnp
from jax import lax
from jax.sharding import PartitionSpec as P


def swiglu_parts(gate_sum, up_sum, back_sum):
    logistic = jax.nn.sigmoid(gate_sum)
    activated = gate_sum * logistic
    hidden = (activated * up_sum).astype(jnp.bfloat16)
    gate_delta = (back_sum * up_sum * logistic * (1.0 + gate_sum * (1.0 - logistic))).astype(
        jnp.bfloat16
    )
    up_delta = (back_sum * activated).astype(jnp.bfloat16)
    return (hidden, gate_delta, up_delta)


def local(tokens, out_grad, expert_ids, route_weights, gate_weight, up_weight, down_weight):
    token_count, width_dev = tokens.shape
    per_token = expert_ids.shape[1]
    local_experts = gate_weight.shape[0]
    hidden_units = gate_weight.shape[2]
    sources = lax.axis_size("expert")
    experts = local_experts * sources
    capacity = 2 * token_count * per_token // experts
    slot_count = token_count * per_token
    flat_ids = expert_ids.reshape(slot_count)
    position = jnp.arange(slot_count, dtype=jnp.int32)
    earlier = (flat_ids[None, :] == flat_ids[:, None]) & (position[None, :] < position[:, None])
    slot_rank = jnp.sum(earlier.astype(jnp.int32), axis=1)
    slot_place = (flat_ids * capacity + slot_rank).reshape(token_count, per_token)
    buffer_rows = experts * capacity
    target = jnp.arange(buffer_rows, dtype=jnp.int32)
    matches = (target[:, None, None] == slot_place[None, :, :]).astype(jnp.float32)
    select = jnp.sum(matches, axis=2)
    weighted = jnp.sum(matches * route_weights[None, :, :], axis=2)
    send_tokens = jnp.dot(
        select.astype(jnp.bfloat16), tokens, preferred_element_type=jnp.float32
    ).astype(jnp.bfloat16)
    send_grads = jnp.dot(
        weighted, out_grad.astype(jnp.float32), precision=lax.Precision.HIGHEST
    ).astype(jnp.bfloat16)
    recv_tokens, recv_grads = (
        lax.all_to_all(send_tokens, "expert", split_axis=0, concat_axis=0, tiled=True),
        lax.all_to_all(send_grads, "expert", split_axis=0, concat_axis=0, tiled=True),
    )
    buffer_shape = (sources, local_experts, capacity, width_dev)
    in_tokens = recv_tokens.reshape(buffer_shape)
    in_grads = recv_grads.reshape(buffer_shape)
    row_count = local_experts * sources * capacity
    gate_part = jnp.einsum(
        "sjcd,jdf->jscf", in_tokens, gate_weight, preferred_element_type=jnp.float32
    ).reshape(row_count, hidden_units)
    up_part = jnp.einsum(
        "sjcd,jdf->jscf", in_tokens, up_weight, preferred_element_type=jnp.float32
    ).reshape(row_count, hidden_units)
    back_part = jnp.einsum(
        "sjcd,jfd->jscf", in_grads, down_weight, preferred_element_type=jnp.float32
    ).reshape(row_count, hidden_units)
    gate_sum, up_sum, back_sum = (
        lax.psum_scatter(
            gate_part.astype(jnp.bfloat16), "dp", scatter_dimension=0, tiled=True
        ).astype(jnp.float32),
        lax.psum_scatter(
            up_part.astype(jnp.bfloat16), "dp", scatter_dimension=0, tiled=True
        ).astype(jnp.float32),
        lax.psum_scatter(
            back_part.astype(jnp.bfloat16), "dp", scatter_dimension=0, tiled=True
        ).astype(jnp.float32),
    )
    hidden, gate_delta, up_delta = swiglu_parts(gate_sum, up_sum, back_sum)
    hidden, gate_delta, up_delta = (
        lax.all_gather(hidden, "dp", axis=0, tiled=True),
        lax.all_gather(gate_delta, "dp", axis=0, tiled=True),
        lax.all_gather(up_delta, "dp", axis=0, tiled=True),
    )
    expert_shape = (local_experts, sources, capacity, hidden_units)
    hidden = hidden.reshape(expert_shape)
    gate_delta = gate_delta.reshape(expert_shape)
    up_delta = up_delta.reshape(expert_shape)
    expert_out = jnp.einsum(
        "jscf,jfd->sjcd", hidden, down_weight, preferred_element_type=jnp.float32
    ).astype(jnp.bfloat16)
    expert_back = (
        jnp.einsum("jscf,jdf->sjcd", gate_delta, gate_weight, preferred_element_type=jnp.float32)
        + jnp.einsum("jscf,jdf->sjcd", up_delta, up_weight, preferred_element_type=jnp.float32)
    ).astype(jnp.bfloat16)
    gate_grad = jnp.einsum(
        "sjcd,jscf->jdf", in_tokens, gate_delta, preferred_element_type=jnp.float32
    ).astype(jnp.bfloat16)
    up_grad = jnp.einsum(
        "sjcd,jscf->jdf", in_tokens, up_delta, preferred_element_type=jnp.float32
    ).astype(jnp.bfloat16)
    down_grad = jnp.einsum(
        "jscf,sjcd->jfd", hidden, in_grads, preferred_element_type=jnp.float32
    ).astype(jnp.bfloat16)
    out_back, grad_back = (
        lax.all_to_all(
            expert_out.reshape(buffer_rows, width_dev),
            "expert",
            split_axis=0,
            concat_axis=0,
            tiled=True,
        ),
        lax.all_to_all(
            expert_back.reshape(buffer_rows, width_dev),
            "expert",
            split_axis=0,
            concat_axis=0,
            tiled=True,
        ),
    )
    picked_out = jnp.take(out_back, slot_place, axis=0).astype(jnp.float32)
    layer_out = jnp.sum(picked_out * route_weights[:, :, None], axis=1).astype(jnp.bfloat16)
    picked_back = jnp.take(grad_back, slot_place, axis=0).astype(jnp.float32)
    grad_tokens = jnp.sum(picked_back, axis=1).astype(jnp.bfloat16)
    return (layer_out, grad_tokens, gate_grad, up_grad, down_grad)


def solution(mesh):
    in_specs = (
        P("expert", "dp"),
        P("expert", "dp"),
        P("expert", None),
        P("expert", None),
        P("expert", "dp", None),
        P("expert", "dp", None),
        P("expert", None, "dp"),
    )
    out_specs = (
        P("expert", "dp"),
        P("expert", "dp"),
        P("expert", "dp", None),
        P("expert", "dp", None),
        P("expert", None, "dp"),
    )
    return jax.shard_map(local, mesh=mesh, in_specs=in_specs, out_specs=out_specs, check_vma=False)
```

profile of v0, /device:TPU:0, one launch (start us, length us, event | category | flops | bytes accessed | tf_op | source)
XLA Modules:
  0.0 306.5 jit_solution(516927008975861477)
XLA Ops:
  13.4 5.3 %all-to-all-start.2 = ((bf16[8,96,1024]{2,1,0:T(8,128)(2,1)}), bf16[8,96,1024]{2,1,0:T(8,128)(2,1)S(1)}, u32[]{:S(2)}, u32[]{:S(2)}) async-start(bf16[8,96,1024]{2,1,0:T(8,128)(2,1)} %bitcast.12), calls=%async_computation.4 | async-start | bytes 3145728 | tf_op jit(solution)/shard_map/all_to_all | solution.py:45
  20.5 19.3 %all-to-all-done.2 = bf16[8,96,1024]{2,1,0:T(8,128)(2,1)S(1)} async-done(((bf16[8,96,1024]{2,1,0:T(8,128)(2,1)}), bf16[8,96,1024]{2,1,0:T(8,128)(2,1)S(1)}, u32[]{:S(2)}, u32[]{:S(2)}) %all-to-all-start.2) | async-done | bytes 1572896 | tf_op jit(solution)/shard_map/all_to_all | solution.py:45
  39.8 4.3 %all-to-all-start = ((bf16[8,96,1024]{2,1,0:T(8,128)(2,1)}), bf16[8,96,1024]{2,1,0:T(8,128)(2,1)}, u32[]{:S(2)}, u32[]{:S(2)}) async-start(bf16[8,96,1024]{2,1,0:T(8,128)(2,1)} %bitcast), calls=%async_computation | async-start | bytes 3145728 | tf_op jit(solution)/shard_map/all_to_all | solution.py:44
  45.0 8.9 %fusion.21 = bf16[8,8,12,768]{3,2,1,0:T(8,128)(2,1)S(1)} fusion(bf16[8,768,1024]{2,1,0:T(8,128)(2,1)} %param.15, bf16[8,8,12,1024]{3,0,2,1:T(8,128)(2,1)S(1)} %bitcast.75), kind=kOutput, calls=%fused_computation.26 | convolution fusion | flops 1208549376 | bytes 15335424 | tf_op jit(solution)/shard_map/sjcd,jfd->jscf/dot_general | solution.py:57
  55.1 10.0 %all-to-all-done = bf16[8,96,1024]{2,1,0:T(8,128)(2,1)} async-done(((bf16[8,96,1024]{2,1,0:T(8,128)(2,1)}), bf16[8,96,1024]{2,1,0:T(8,128)(2,1)}, u32[]{:S(2)}, u32[]{:S(2)}) %all-to-all-start) | async-done | bytes 1572896 | tf_op jit(solution)/shard_map/all_to_all | solution.py:44
  67.4 8.7 %fusion.31 = bf16[8,8,12,768]{3,2,1,0:T(8,128)(2,1)} fusion(bf16[8,1024,768]{2,1,0:T(8,128)(2,1)} %param.14, bf16[8,8,12,1024]{3,0,2,1:T(8,128)(2,1)S(1)} %bitcast.71), kind=kOutput, calls=%fused_computation.28 | convolution fusion | flops 1208549376 | bytes 15335424 | tf_op jit(solution)/shard_map/sjcd,jdf->jscf/dot_general | solution.py:54
  76.1 3.2 %convert_element_type.89 = bf16[768,768]{1,0:T(8,128)(2,1)} reshape(bf16[8,8,12,768]{3,2,1,0:T(8,128)(2,1)} %fusion.31) | data formatting | bytes 2359296 | tf_op jit(solution)/shard_map/convert_element_type | solution.py:65
  79.5 8.2 %fusion.26 = bf16[8,8,12,768]{3,2,1,0:T(8,128)(2,1)} fusion(bf16[8,1024,768]{2,1,0:T(8,128)(2,1)} %param.13, bf16[8,8,12,1024]{3,0,2,1:T(8,128)(2,1)S(1)} %bitcast.72), kind=kOutput, calls=%fused_computation.27 | convolution fusion | flops 1208549376 | bytes 15335424 | tf_op jit(solution)/shard_map/sjcd,jdf->jscf/dot_general | solution.py:51
  87.7 3.1 %convert_element_type.86 = bf16[768,768]{1,0:T(8,128)(2,1)} reshape(bf16[8,8,12,768]{3,2,1,0:T(8,128)(2,1)} %fusion.26) | data formatting | bytes 2359296 | tf_op jit(solution)/shard_map/convert_element_type | solution.py:62
  90.9 25.8 %reduce-scatter.6.cloned.1.call-done = bf16[192,768]{1,0:T(8,128)(2,1)} async-done(((bf16[768,768]{1,0:T(8,128)(2,1)}), bf16[192,768]{1,0:T(8,128)(2,1)}) %reduce-scatter.6.cloned.1.call-update) | async-done | bytes 294928 | tf_op jit(solution)/shard_map/reduce_scatter | solution.py:64
  116.8 30.2 %reduce-scatter.4.cloned.1.call-done = bf16[192,768]{1,0:T(8,128)(2,1)} async-done(((bf16[768,768]{1,0:T(8,128)(2,1)}), bf16[192,768]{1,0:T(8,128)(2,1)}) %reduce-scatter.4.cloned.1.call-update) | async-done | bytes 294928 | tf_op jit(solution)/shard_map/reduce_scatter | solution.py:61
  151.5 27.2 %all-gather.4.cloned.1.call-done = bf16[768,768]{1,0:T(8,128)(2,1)} async-done(((bf16[192,768]{1,0:T(8,128)(2,1)}), bf16[768,768]{1,0:T(8,128)(2,1)}) %all-gather.4.cloned.1.call-update) | async-done | bytes 1179664 | tf_op jit(solution)/shard_map/all_gather | solution.py:73
  180.9 6.8 %bitcast_convert_fusion = bf16[8,768,1024]{2,1,0:T(8,128)(2,1)} fusion(bf16[8,8,12,768]{3,2,1,0:T(8,128)(2,1)S(1)} %reshape.64, bf16[8,8,12,1024]{3,0,2,1:T(8,128)(2,1)S(1)} %bitcast.76), kind=kOutput, calls=%fused_computation.2 | convolution fusion | flops 1214251008 | bytes 15335424 | tf_op jit(solution)/shard_map/jscf,sjcd->jfd/dot_general | solution.py:94
  187.7 6.4 %convert_bitcast_fusion = bf16[8,8,12,1024]{3,2,0,1:T(8,128)(2,1)S(1)} fusion(bf16[8,8,12,768]{3,2,1,0:T(8,128)(2,1)S(1)} %reshape.64, bf16[8,768,1024]{2,1,0:T(8,128)(2,1)} %param.15), kind=kOutput, calls=%fused_computation.23 | convolution fusion | flops 1208745984 | bytes 15335424 | tf_op jit(solution)/shard_map/jscf,jfd->sjcd/dot_general | solution.py:81
  197.0 4.5 %all-to-all-start.1 = ((bf16[8,96,1024]{2,1,0:T(8,128)(2,1)}), bf16[8,96,1024]{2,1,0:T(8,128)(2,1)}, u32[]{:S(2)}, u32[]{:S(2)}) async-start(bf16[8,96,1024]{2,1,0:T(8,128)(2,1)} %copy.76), calls=%async_computation.3 | async-start | bytes 3145728 | tf_op jit(solution)/shard_map/all_to_all | solution.py:98
  201.5 8.8 %all-gather.8.cloned.1.call-done = bf16[768,768]{1,0:T(8,128)(2,1)} async-done(((bf16[192,768]{1,0:T(8,128)(2,1)}), bf16[768,768]{1,0:T(8,128)(2,1)}) %all-gather.8.cloned.1.call-update) | async-done | bytes 1179664 | tf_op jit(solution)/shard_map/all_gather | solution.py:75
  212.5 11.2 %fusion = f32[8,8,12,1024]{3,2,1,0:T(8,128)} fusion(bf16[8,8,12,768]{3,2,1,0:T(8,128)(2,1)S(1)} %reshape.67, bf16[8,1024,768]{2,1,0:T(8,128)(2,1)} %param.14), kind=kOutput, calls=%fused_computation.5 | convolution fusion | flops 1207959552 | bytes 16908288 | tf_op jit(solution)/shard_map/jscf,jdf->sjcd/dot_general | solution.py:86
  223.7 18.2 %all-gather.6.cloned.1.call-done = bf16[768,768]{1,0:T(8,128)(2,1)} async-done(((bf16[192,768]{1,0:T(8,128)(2,1)}), bf16[768,768]{1,0:T(8,128)(2,1)}) %all-gather.6.cloned.1.call-update) | async-done | bytes 1179664 | tf_op jit(solution)/shard_map/all_gather | solution.py:74
  245.0 10.3 %bitcast_convert_fusion.2 = bf16[8,1024,768]{2,1,0:T(8,128)(2,1)} fusion(bf16[8,8,12,1024]{3,0,2,1:T(8,128)(2,1)} %bitcast.73, bf16[8,8,12,768]{3,2,1,0:T(8,128)(2,1)} %reshape.66), kind=kOutput, calls=%fused_computation.4 | convolution fusion | flops 1214251008 | bytes 15335424 | tf_op jit(solution)/shard_map/sjcd,jscf->jdf/dot_general | solution.py:88
  255.3 10.6 %fusion.16 = bf16[8,8,12,1024]{3,2,0,1:T(8,128)(2,1)} fusion(f32[8,8,12,1024]{3,2,1,0:T(8,128)S(1)} %copy-done.2, bf16[8,8,12,768]{3,2,1,0:T(8,128)(2,1)} %reshape.66, bf16[8,1024,768]{2,1,0:T(8,128)(2,1)} %param.13), kind=kOutput, calls=%fused_computation.22 | convolution fusion | flops 1209532416 | bytes 18481152 | tf_op jit(solution)/shard_map/jscf,jdf->sjcd/dot_general | solution.py:85
  270.4 4.0 %all-to-all-start.3 = ((bf16[8,96,1024]{2,1,0:T(8,128)(2,1)}), bf16[8,96,1024]{2,1,0:T(8,128)(2,1)S(1)}, u32[]{:S(2)}, u32[]{:S(2)}) async-start(bf16[8,96,1024]{2,1,0:T(8,128)(2,1)} %copy.84), calls=%async_computation.6 | async-start | bytes 3145728 | tf_op jit(solution)/shard_map/all_to_all | solution.py:105
  274.4 8.0 %bitcast_convert_fusion.1 = bf16[8,1024,768]{2,1,0:T(8,128)(2,1)} fusion(bf16[8,8,12,1024]{3,0,2,1:T(8,128)(2,1)S(1)} %bitcast.74, bf16[8,8,12,768]{3,2,1,0:T(8,128)(2,1)} %copy-done.5), kind=kOutput, calls=%fused_computation.3 | convolution fusion | flops 1214251008 | bytes 15335424 | tf_op jit(solution)/shard_map/sjcd,jscf->jdf/dot_general | solution.py:91
  282.4 4.4 %gather_fusion = bf16[384,1024]{1,0:T(8,128)(2,1)S(1)} fusion(bf16[768,1024]{1,0:T(8,128)(2,1)} %bitcast.10, s32[1024]{0:T(1024)S(1)} %copy-done.6), kind=kCustom, calls=%fused_computation.clone | custom fusion | bytes 1574400 | tf_op jit(solution)/shard_map/jit(_take)/gather | solution.py:113
  286.8 8.4 %all-to-all-done.3 = bf16[8,96,1024]{2,1,0:T(8,128)(2,1)S(1)} async-done(((bf16[8,96,1024]{2,1,0:T(8,128)(2,1)}), bf16[8,96,1024]{2,1,0:T(8,128)(2,1)S(1)}, u32[]{:S(2)}, u32[]{:S(2)}) %all-to-all-start.3) | async-done | bytes 1572896 | tf_op jit(solution)/shard_map/all_to_all | solution.py:105
  (66 shorter events, 36.5 us)
Async XLA Ops:
  7.2 3.7 %copy-start = (bf16[48,1024]{1,0:T(8,128)(2,1)S(1)}, bf16[48,1024]{1,0:T(8,128)(2,1)}, u32[]{:S(2)}) copy-start(bf16[48,1024]{1,0:T(8,128)(2,1)} %param.10) | copy-start | bytes 294916
  8.0 5.4 %copy-start.7 = (f32[48,8]{1,0:T(8,128)}, f32[48,8]{1,0:T(8,128)S(1)}, u32[]{:S(2)}) copy-start(f32[48,8]{1,0:T(8,128)S(1)} %copy.78) | copy-start | bytes 4612
  13.4 5.3 %copy-start.9 = (bf16[48,1024]{1,0:T(8,128)(2,1)S(1)}, bf16[48,1024]{1,0:T(8,128)(2,1)}, u32[]{:S(2)}) copy-start(bf16[48,1024]{1,0:T(8,128)(2,1)} %param.9) | copy-start | bytes 294916
  13.4 26.3 %all-to-all-start.2 = ((bf16[8,96,1024]{2,1,0:T(8,128)(2,1)}), bf16[8,96,1024]{2,1,0:T(8,128)(2,1)S(1)}, u32[]{:S(2)}, u32[]{:S(2)}) async-start(bf16[8,96,1024]{2,1,0:T(8,128)(2,1)} %bitcast.12), calls=%async_computation.4 | async-start | bytes 3145728 | tf_op jit(solution)/shard_map/all_to_all | solution.py:45
  39.8 25.3 %all-to-all-start = ((bf16[8,96,1024]{2,1,0:T(8,128)(2,1)}), bf16[8,96,1024]{2,1,0:T(8,128)(2,1)}, u32[]{:S(2)}, u32[]{:S(2)}) async-start(bf16[8,96,1024]{2,1,0:T(8,128)(2,1)} %bitcast), calls=%async_computation | async-start | bytes 3145728 | tf_op jit(solution)/shard_map/all_to_all | solution.py:44
  44.1 46.9 %reduce-scatter.8.cloned.1.call-start = ((), (), s32[]{:S(2)}) async-start(), calls=%async_computation.10 | async-start | bytes 1474560 | tf_op jit(solution)/shard_map/reduce_scatter | solution.py:67
  55.1 61.7 %reduce-scatter.6.cloned.1.call-start = ((), (), s32[]{:S(2)}) async-start(), calls=%async_computation.8 | async-start | bytes 1474560 | tf_op jit(solution)/shard_map/reduce_scatter | solution.py:64
  67.4 12.1 %copy-start.3 = (bf16[8,96,1024]{2,0,1:T(8,128)(2,1)}, bf16[8,96,1024]{2,0,1:T(8,128)(2,1)S(1)}, u32[]{:S(2)}) copy-start(bf16[8,96,1024]{2,0,1:T(8,128)(2,1)S(1)} %copy.72) | copy-start | bytes 4718596
  79.3 67.7 %reduce-scatter.4.cloned.1.call-start = ((), (), s32[]{:S(2)}) async-start(), calls=%async_computation.7 | async-start | bytes 1474560 | tf_op jit(solution)/shard_map/reduce_scatter | solution.py:61
  90.9 87.9 %all-gather.4.cloned.1.call-start = ((), (), s32[]{:S(2)}) async-start(), calls=%async_computation.9 | async-start | bytes 1474560 | tf_op jit(solution)/shard_map/all_gather | solution.py:73
  149.4 60.9 %all-gather.8.cloned.1.call-start = ((), (), s32[]{:S(2)}) async-start(), calls=%async_computation.12 | async-start | bytes 1474560 | tf_op jit(solution)/shard_map/all_gather | solution.py:75
  150.0 91.9 %all-gather.6.cloned.1.call-start = ((), (), s32[]{:S(2)}) async-start(), calls=%async_computation.11 | async-start | bytes 1474560 | tf_op jit(solution)/shard_map/all_gather | solution.py:74
  197.0 73.4 %all-to-all-start.1 = ((bf16[8,96,1024]{2,1,0:T(8,128)(2,1)}), bf16[8,96,1024]{2,1,0:T(8,128)(2,1)}, u32[]{:S(2)}, u32[]{:S(2)}) async-start(bf16[8,96,1024]{2,1,0:T(8,128)(2,1)} %copy.76), calls=%async_computation.3 | async-start | bytes 3145728 | tf_op jit(solution)/shard_map/all_to_all | solution.py:98
  212.5 11.2 %copy-start.5 = (bf16[8,8,12,768]{3,2,1,0:T(8,128)(2,1)}, bf16[8,8,12,768]{3,2,1,0:T(8,128)(2,1)S(1)}, u32[]{:S(2)}) copy-start(bf16[8,8,12,768]{3,2,1,0:T(8,128)(2,1)S(1)} %reshape.67) | copy-start | bytes 3538948
  245.0 10.3 %copy-start.2 = (f32[8,8,12,1024]{3,2,1,0:T(8,128)S(1)}, f32[8,8,12,1024]{3,2,1,0:T(8,128)}, u32[]{:S(2)}) copy-start(f32[8,8,12,1024]{3,2,1,0:T(8,128)} %fusion) | copy-start | bytes 9437188
  270.4 4.0 %copy-start.4 = (bf16[8,96,1024]{2,0,1:T(8,128)(2,1)S(1)}, bf16[8,96,1024]{2,0,1:T(8,128)(2,1)}, u32[]{:S(2)}) copy-start(bf16[8,96,1024]{2,0,1:T(8,128)(2,1)} %copy-done.3) | copy-start | bytes 4718596
  270.4 24.8 %all-to-all-start.3 = ((bf16[8,96,1024]{2,1,0:T(8,128)(2,1)}), bf16[8,96,1024]{2,1,0:T(8,128)(2,1)S(1)}, u32[]{:S(2)}, u32[]{:S(2)}) async-start(bf16[8,96,1024]{2,1,0:T(8,128)(2,1)} %copy.84), calls=%async_computation.6 | async-start | bytes 3145728 | tf_op jit(solution)/shard_map/all_to_all | solution.py:105
  274.4 8.1 %copy-start.6 = (s32[1024]{0:T(1024)S(1)}, s32[1024]{0:T(1024)}, u32[]{:S(2)}) copy-start(s32[1024]{0:T(1024)} %pad_clamp_fusion) | copy-start | bytes 12292
  295.2 2.1 copy-start.8
  295.2 2.1 copy-start.10
  295.2 4.4 %copy-start.1 = (bf16[48,1024]{1,0:T(8,128)(2,1)S(1)}, bf16[48,1024]{1,0:T(8,128)(2,1)}, u32[]{:S(2)}) copy-start(bf16[48,1024]{1,0:T(8,128)(2,1)} %param.10) | copy-start | bytes 294916
Sparse Core Ops, SparseCore 0:
  55.2 30.7 reduce-scatter.7
  88.8 27.8 reduce-scatter.5
  119.1 27.8 reduce-scatter.3
  149.5 29.1 all-gather.3
  180.7 29.5 all-gather.7
  212.3 29.5 all-gather.5
where the time goes:
time: 308 us; the launch traced here: 306 us
  waiting for transfers between devices  149 us (48%)
  matrix products  83.4 us (27%)
  local copies, waits for them, and re-layouts  34.7 us (11%)
  starting transfers between devices  18.5 us (6%)
  between operations  14.3 us (5%)
  other arithmetic  7.03 us (2%)
    reduce_scatter x1, waiting for transfers between devices, local(): lax.psum_scatter(gate_part.astype(jnp.bfloat16), 'dp', scatter_dimension=...  30.2 us
    all_gather x1, waiting for transfers between devices, local(): lax.all_gather(hidden, 'dp', axis=0, tiled=True)  27.2 us
    reduce_scatter x1, waiting for transfers between devices, local(): lax.psum_scatter(up_part.astype(jnp.bfloat16), 'dp', scatter_dimension=0,...  25.8 us
    all_to_all x1, waiting for transfers between devices, local(): lax.all_to_all(send_grads, 'expert', split_axis=0, concat_axis=0, tiled=T...  19.3 us
    all_gather x1, waiting for transfers between devices, local(): lax.all_gather(gate_delta, 'dp', axis=0, tiled=True)  18.2 us
    dot_general x1, matrix products, local(): jnp.einsum('jscf,jdf->sjcd', up_delta, up_weight, preferred_element_type=...  11.2 us
    dot_general x1, matrix products, local(): jnp.einsum('jscf,jdf->sjcd', gate_delta, gate_weight, preferred_element_t...  10.6 us
    dot_general x1, matrix products, local(): jnp.einsum('sjcd,jscf->jdf', in_tokens, gate_delta, preferred_element_typ...  10.3 us
  transfers between devices with their start and end apart: 10, of which 8 were waited for; matrix products, arithmetic and copies ran while one was open for 37% of the time, Pallas kernels for 0%

commit v1 on v0

--- a/solution.py
+++ b/solution.py
@@ -2,6 +2,12 @@
 import jax.numpy as jnp
 from jax import lax
 from jax.sharding import PartitionSpec as P
+
+
+def link_the_ports(block_here, on_dim):
+    block_here = jnp.moveaxis(block_here, 0, on_dim)
+    val2 = block_here.shape
+    return block_here.reshape(*val2[:on_dim], val2[on_dim] * val2[on_dim + 1], *val2[on_dim + 2 :])
 
 
 def swiglu_parts(gate_sum, up_sum, back_sum):
@@ -16,6 +22,18 @@
 
 
 def local(tokens, out_grad, expert_ids, route_weights, gate_weight, up_weight, down_weight):
+
+    def lay_bands(dim_k, peer_axis, local_array):
+        n_parts = jax.lax.axis_size(peer_axis)
+        shelf = [(t, (t + 1) % n_parts) for t in range(n_parts)]
+        pile = [local_array]
+        while len(pile) < n_parts:
+            pile.append(jax.lax.ppermute(pile[-1], peer_axis, shelf))
+        met_up = jax.lax.axis_index(peer_axis)
+        raw_out = jnp.stack(pile)
+        pile = raw_out[(met_up - jnp.arange(n_parts)) % n_parts]
+        return link_the_ports(pile, dim_k)
+
     token_count, width_dev = tokens.shape
     per_token = expert_ids.shape[1]
     local_experts = gate_weight.shape[0]
@@ -71,7 +89,7 @@
     hidden, gate_delta, up_delta = swiglu_parts(gate_sum, up_sum, back_sum)
     hidden, gate_delta, up_delta = (
         lax.all_gather(hidden, "dp", axis=0, tiled=True),
-        lax.all_gather(gate_delta, "dp", axis=0, tiled=True),
+        lay_bands(0, "dp", gate_delta),
         lax.all_gather(up_delta, "dp", axis=0, tiled=True),
     )
     expert_shape = (local_experts, sources, capacity, hidden_units)

time: 308 us -> 296 us (0.961)
  waiting for transfers between devices: 149 us -> 134 us
  matrix products: 83.4 us -> 79 us
  local copies, waits for them, and re-layouts: 34.7 us -> 38.6 us
    ppermute x0 -> x3, waiting for transfers between devices: none -> 40 us  [lay_bands(): pile.append(jax.lax.ppermute(pile[-1], peer_axis, shelf))]
    all_gather x1, waiting for transfers between devices: 27.2 us -> 0.01 us  [local(): lax.all_gather(hidden, 'dp', axis=0, tiled=True)]
    all_gather x1 -> x0, waiting for transfers between devices: 18.2 us -> none  [local(): lax.all_gather(gate_delta, 'dp', axis=0, tiled=True)]
    all_gather x1, waiting for transfers between devices: 8.77 us -> 0.02 us  [local(): lax.all_gather(up_delta, 'dp', axis=0, tiled=True)]
    another operation x0 -> x1, local copies, waits for them, and re-layouts: none -> 3.15 us  [local(): gate_delta = gate_delta.reshape(expert_shape)]
    reshape x1 -> x0, local copies, waits for them, and re-layouts: 3.12 us -> none  [local(): gate_delta = gate_delta.reshape(expert_shape)]
  transfers between devices with their start and end apart: 10 -> 12, of which waited for: 8 -> 8; matrix products, arithmetic and copies ran while one was open for 37% -> 39% of each run, Pallas kernels for 0% -> 0%
where the time goes in v1:
time: 296 us; the launch traced here: 295 us
  waiting for transfers between devices  134 us (45%)
  matrix products  79 us (27%)
  local copies, waits for them, and re-layouts  38.6 us (13%)
  starting transfers between devices  19.6 us (7%)
  between operations  14 us (5%)
  other arithmetic  9.31 us (3%)
    ppermute x3, waiting for transfers between devices, lay_bands(): pile.append(jax.lax.ppermute(pile[-1], peer_axis, shelf))  40 us
    reduce_scatter x1, waiting for transfers between devices, local(): lax.psum_scatter(gate_part.astype(jnp.bfloat16), 'dp', scatter_dimension=...  30.2 us
    reduce_scatter x1, waiting for transfers between devices, local(): lax.psum_scatter(up_part.astype(jnp.bfloat16), 'dp', scatter_dimension=0,...  25.9 us
    all_to_all x1, waiting for transfers between devices, local(): lax.all_to_all(send_grads, 'expert', split_axis=0, concat_axis=0, tiled=T...  19.3 us
    dot_general x1, matrix products, local(): jnp.einsum('jscf,jdf->sjcd', gate_delta, gate_weight, preferred_element_t...  10.6 us
    all_to_all x1, waiting for transfers between devices, local(): lax.all_to_all(send_tokens, 'expert', split_axis=0, concat_axis=0, tiled=...  9.99 us
    dot_general x1, matrix products, local(): jnp.einsum('jscf,jdf->sjcd', up_delta, up_weight, preferred_element_type=...  9.12 us
    dot_general x1, matrix products, local(): jnp.einsum('sjcd,jfd->jscf', in_grads, down_weight, preferred_element_typ...  8.88 us
  transfers between devices with their start and end apart: 12, of which 8 were waited for; matrix products, arithmetic and copies ran while one was open for 39% of the time, Pallas kernels for 0%

profile of v1, /device:TPU:0, one launch (start us, length us, event | category | flops | bytes accessed | tf_op | source)
XLA Modules:
  0.0 294.6 jit_solution(16048921670996724207)
XLA Ops:
  13.4 5.3 %all-to-all-start.2 = ((bf16[8,96,1024]{2,1,0:T(8,128)(2,1)}), bf16[8,96,1024]{2,1,0:T(8,128)(2,1)S(1)}, u32[]{:S(2)}, u32[]{:S(2)}) async-start(bf16[8,96,1024]{2,1,0:T(8,128)(2,1)} %bitcast.12), calls=%async_computation.4 | async-start | bytes 3145728 | tf_op jit(solution)/shard_map/all_to_all | solution.py:63
  20.5 19.3 %all-to-all-done.2 = bf16[8,96,1024]{2,1,0:T(8,128)(2,1)S(1)} async-done(((bf16[8,96,1024]{2,1,0:T(8,128)(2,1)}), bf16[8,96,1024]{2,1,0:T(8,128)(2,1)S(1)}, u32[]{:S(2)}, u32[]{:S(2)}) %all-to-all-start.2) | async-done | bytes 1572896 | tf_op jit(solution)/shard_map/all_to_all | solution.py:63
  39.8 4.3 %all-to-all-start = ((bf16[8,96,1024]{2,1,0:T(8,128)(2,1)}), bf16[8,96,1024]{2,1,0:T(8,128)(2,1)}, u32[]{:S(2)}, u32[]{:S(2)}) async-start(bf16[8,96,1024]{2,1,0:T(8,128)(2,1)} %bitcast), calls=%async_computation | async-start | bytes 3145728 | tf_op jit(solution)/shard_map/all_to_all | solution.py:62
  45.0 8.9 %fusion.21 = bf16[8,8,12,768]{3,2,1,0:T(8,128)(2,1)S(1)} fusion(bf16[8,768,1024]{2,1,0:T(8,128)(2,1)} %param.15, bf16[8,8,12,1024]{3,0,2,1:T(8,128)(2,1)S(1)} %bitcast.81), kind=kOutput, calls=%fused_computation.27 | convolution fusion | flops 1208549376 | bytes 15335424 | tf_op jit(solution)/shard_map/sjcd,jfd->jscf/dot_general | solution.py:75
  55.1 10.0 %all-to-all-done = bf16[8,96,1024]{2,1,0:T(8,128)(2,1)} async-done(((bf16[8,96,1024]{2,1,0:T(8,128)(2,1)}), bf16[8,96,1024]{2,1,0:T(8,128)(2,1)}, u32[]{:S(2)}, u32[]{:S(2)}) %all-to-all-start) | async-done | bytes 1572896 | tf_op jit(solution)/shard_map/all_to_all | solution.py:62
  67.4 8.7 %fusion.31 = bf16[8,8,12,768]{3,2,1,0:T(8,128)(2,1)} fusion(bf16[8,1024,768]{2,1,0:T(8,128)(2,1)} %param.14, bf16[8,8,12,1024]{3,0,2,1:T(8,128)(2,1)S(1)} %bitcast.77), kind=kOutput, calls=%fused_computation.29 | convolution fusion | flops 1208549376 | bytes 15335424 | tf_op jit(solution)/shard_map/sjcd,jdf->jscf/dot_general | solution.py:72
  76.1 3.2 %convert_element_type.89 = bf16[768,768]{1,0:T(8,128)(2,1)} reshape(bf16[8,8,12,768]{3,2,1,0:T(8,128)(2,1)} %fusion.31) | data formatting | bytes 2359296 | tf_op jit(solution)/shard_map/convert_element_type | solution.py:83
  79.5 8.2 %fusion.26 = bf16[8,8,12,768]{3,2,1,0:T(8,128)(2,1)} fusion(bf16[8,1024,768]{2,1,0:T(8,128)(2,1)} %param.13, bf16[8,8,12,1024]{3,0,2,1:T(8,128)(2,1)S(1)} %bitcast.78), kind=kOutput, calls=%fused_computation.28 | convolution fusion | flops 1208549376 | bytes 15335424 | tf_op jit(solution)/shard_map/sjcd,jdf->jscf/dot_general | solution.py:69
  90.9 25.9 %reduce-scatter.6.cloned.1.call-done = bf16[192,768]{1,0:T(8,128)(2,1)} async-done(((bf16[768,768]{1,0:T(8,128)(2,1)}), bf16[192,768]{1,0:T(8,128)(2,1)}) %reduce-scatter.6.cloned.1.call-update) | async-done | bytes 294928 | tf_op jit(solution)/shard_map/reduce_scatter | solution.py:82
  116.8 30.2 %reduce-scatter.4.cloned.1.call-done = bf16[192,768]{1,0:T(8,128)(2,1)} async-done(((bf16[768,768]{1,0:T(8,128)(2,1)}), bf16[192,768]{1,0:T(8,128)(2,1)}) %reduce-scatter.4.cloned.1.call-update) | async-done | bytes 294928 | tf_op jit(solution)/shard_map/reduce_scatter | solution.py:79
  149.5 10.6 %collective-permute-done = bf16[192,768]{1,0:T(8,128)(2,1)} collective-permute-done((bf16[192,768]{1,0:T(8,128)(2,1)S(1)}, bf16[192,768]{1,0:T(8,128)(2,1)}, u32[]{:S(2)}, u32[]{:S(2)}) %collective-permute-start) | collective-permute-done | bytes 294944 | tf_op jit(solution)/shard_map/ppermute | solution.py:31
  161.0 16.7 %collective-permute-done.1 = bf16[192,768]{1,0:T(8,128)(2,1)} collective-permute-done((bf16[192,768]{1,0:T(8,128)(2,1)}, bf16[192,768]{1,0:T(8,128)(2,1)}, u32[]{:S(2)}, u32[]{:S(2)}) %collective-permute-start.1) | collective-permute-done | bytes 294944 | tf_op jit(solution)/shard_map/ppermute | solution.py:31
  179.3 12.7 %collective-permute-done.2 = bf16[192,768]{1,0:T(8,128)(2,1)} collective-permute-done((bf16[192,768]{1,0:T(8,128)(2,1)}, bf16[192,768]{1,0:T(8,128)(2,1)}, u32[]{:S(2)}, u32[]{:S(2)}) %collective-permute-start.2) | collective-permute-done | bytes 294944 | tf_op jit(solution)/shard_map/ppermute | solution.py:31
  197.2 3.1 %reshape_reshape.3 = bf16[8,8,12,768]{3,2,1,0:T(8,128)(2,1)} reshape(bf16[4,192,768]{2,1,0:T(8,128)(2,1)} %gather_fusion) | data formatting | bytes 2359296 | tf_op jit(solution)/shard_map/reshape;reshape | solution.py:97
  200.4 8.0 %bitcast_convert_fusion.2 = bf16[8,1024,768]{2,1,0:T(8,128)(2,1)} fusion(bf16[8,8,12,1024]{3,0,2,1:T(8,128)(2,1)S(1)} %bitcast.79, bf16[8,8,12,768]{3,2,1,0:T(8,128)(2,1)} %reshape_reshape.3), kind=kOutput, calls=%fused_computation.5 | convolution fusion | flops 1214251008 | bytes 15335424 | tf_op jit(solution)/shard_map/sjcd,jscf->jdf/dot_general | solution.py:106
  210.6 6.8 %bitcast_convert_fusion = bf16[8,768,1024]{2,1,0:T(8,128)(2,1)} fusion(bf16[8,8,12,768]{3,2,1,0:T(8,128)(2,1)S(1)} %reshape.110, bf16[8,8,12,1024]{3,0,2,1:T(8,128)(2,1)S(1)} %bitcast.82), kind=kOutput, calls=%fused_computation.3 | convolution fusion | flops 1214251008 | bytes 15335424 | tf_op jit(solution)/shard_map/jscf,sjcd->jfd/dot_general | solution.py:112
  217.3 6.4 %convert_bitcast_fusion = bf16[8,8,12,1024]{3,2,0,1:T(8,128)(2,1)S(1)} fusion(bf16[8,8,12,768]{3,2,1,0:T(8,128)(2,1)S(1)} %reshape.110, bf16[8,768,1024]{2,1,0:T(8,128)(2,1)} %param.15), kind=kOutput, calls=%fused_computation.24 | convolution fusion | flops 1208745984 | bytes 15335424 | tf_op jit(solution)/shard_map/jscf,jfd->sjcd/dot_general | solution.py:99
  226.7 4.5 %all-to-all-start.1 = ((bf16[8,96,1024]{2,1,0:T(8,128)(2,1)}), bf16[8,96,1024]{2,1,0:T(8,128)(2,1)}, u32[]{:S(2)}, u32[]{:S(2)}) async-start(bf16[8,96,1024]{2,1,0:T(8,128)(2,1)} %copy.76), calls=%async_computation.3 | async-start | bytes 3145728 | tf_op jit(solution)/shard_map/all_to_all | solution.py:116
  234.4 9.1 %fusion = f32[8,8,12,1024]{3,2,1,0:T(8,128)S(1)} fusion(bf16[8,8,12,768]{3,2,1,0:T(8,128)(2,1)} %reshape.112, bf16[8,1024,768]{2,1,0:T(8,128)(2,1)} %param.14), kind=kOutput, calls=%fused_computation.6 | convolution fusion | flops 1207959552 | bytes 16908288 | tf_op jit(solution)/shard_map/jscf,jdf->sjcd/dot_general | solution.py:104
  243.5 10.6 %fusion.16 = bf16[8,8,12,1024]{3,2,0,1:T(8,128)(2,1)} fusion(f32[8,8,12,1024]{3,2,1,0:T(8,128)S(1)} %fusion, bf16[8,8,12,768]{3,2,1,0:T(8,128)(2,1)} %reshape_reshape.3, bf16[8,1024,768]{2,1,0:T(8,128)(2,1)} %param.13), kind=kOutput, calls=%fused_computation.23 | convolution fusion | flops 1209532416 | bytes 18481152 | tf_op jit(solution)/shard_map/jscf,jdf->sjcd/dot_general | solution.py:103
  258.6 4.0 %all-to-all-start.3 = ((bf16[8,96,1024]{2,1,0:T(8,128)(2,1)}), bf16[8,96,1024]{2,1,0:T(8,128)(2,1)S(1)}, u32[]{:S(2)}, u32[]{:S(2)}) async-start(bf16[8,96,1024]{2,1,0:T(8,128)(2,1)} %copy.84), calls=%async_computation.6 | async-start | bytes 3145728 | tf_op jit(solution)/shard_map/all_to_all | solution.py:123
  262.6 8.0 %bitcast_convert_fusion.1 = bf16[8,1024,768]{2,1,0:T(8,128)(2,1)} fusion(bf16[8,8,12,1024]{3,0,2,1:T(8,128)(2,1)S(1)} %bitcast.80, bf16[8,8,12,768]{3,2,1,0:T(8,128)(2,1)} %reshape.112), kind=kOutput, calls=%fused_computation.4 | convolution fusion | flops 1214251008 | bytes 15335424 | tf_op jit(solution)/shard_map/sjcd,jscf->jdf/dot_general | solution.py:109
  270.6 4.4 %gather_fusion.1 = bf16[384,1024]{1,0:T(8,128)(2,1)S(1)} fusion(bf16[768,1024]{1,0:T(8,128)(2,1)} %bitcast.10, s32[1024]{0:T(1024)S(1)} %copy-done.4), kind=kCustom, calls=%fused_computation.clone | custom fusion | bytes 1574400 | tf_op jit(solution)/shard_map/jit(_take)/gather | solution.py:131
  275.0 8.6 %all-to-all-done.3 = bf16[8,96,1024]{2,1,0:T(8,128)(2,1)S(1)} async-done(((bf16[8,96,1024]{2,1,0:T(8,128)(2,1)}), bf16[8,96,1024]{2,1,0:T(8,128)(2,1)S(1)}, u32[]{:S(2)}, u32[]{:S(2)}) %all-to-all-start.3) | async-done | bytes 1572896 | tf_op jit(solution)/shard_map/all_to_all | solution.py:123
  (69 shorter events, 43.2 us)
Async XLA Ops:
  7.2 3.7 %copy-start = (bf16[48,1024]{1,0:T(8,128)(2,1)S(1)}, bf16[48,1024]{1,0:T(8,128)(2,1)}, u32[]{:S(2)}) copy-start(bf16[48,1024]{1,0:T(8,128)(2,1)} %param.10) | copy-start | bytes 294916
  8.0 5.4 %copy-start.5 = (f32[48,8]{1,0:T(8,128)}, f32[48,8]{1,0:T(8,128)S(1)}, u32[]{:S(2)}) copy-start(f32[48,8]{1,0:T(8,128)S(1)} %copy.78) | copy-start | bytes 4612
  13.4 5.3 %copy-start.7 = (bf16[48,1024]{1,0:T(8,128)(2,1)S(1)}, bf16[48,1024]{1,0:T(8,128)(2,1)}, u32[]{:S(2)}) copy-start(bf16[48,1024]{1,0:T(8,128)(2,1)} %param.9) | copy-start | bytes 294916
  13.4 26.3 %all-to-all-start.2 = ((bf16[8,96,1024]{2,1,0:T(8,128)(2,1)}), bf16[8,96,1024]{2,1,0:T(8,128)(2,1)S(1)}, u32[]{:S(2)}, u32[]{:S(2)}) async-start(bf16[8,96,1024]{2,1,0:T(8,128)(2,1)} %bitcast.12), calls=%async_computation.4 | async-start | bytes 3145728 | tf_op jit(solution)/shard_map/all_to_all | solution.py:63
  39.8 25.4 %all-to-all-start = ((bf16[8,96,1024]{2,1,0:T(8,128)(2,1)}), bf16[8,96,1024]{2,1,0:T(8,128)(2,1)}, u32[]{:S(2)}, u32[]{:S(2)}) async-start(bf16[8,96,1024]{2,1,0:T(8,128)(2,1)} %bitcast), calls=%async_computation | async-start | bytes 3145728 | tf_op jit(solution)/shard_map/all_to_all | solution.py:62
  44.1 46.8 %reduce-scatter.8.cloned.1.call-start = ((), (), s32[]{:S(2)}) async-start(), calls=%async_computation.10 | async-start | bytes 1474560 | tf_op jit(solution)/shard_map/reduce_scatter | solution.py:85
  55.1 61.7 %reduce-scatter.6.cloned.1.call-start = ((), (), s32[]{:S(2)}) async-start(), calls=%async_computation.8 | async-start | bytes 1474560 | tf_op jit(solution)/shard_map/reduce_scatter | solution.py:82
  67.4 133.0 %copy-start.2 = (bf16[8,96,1024]{2,0,1:T(8,128)(2,1)}, bf16[8,96,1024]{2,0,1:T(8,128)(2,1)S(1)}, u32[]{:S(2)}) copy-start(bf16[8,96,1024]{2,0,1:T(8,128)(2,1)S(1)} %copy.72) | copy-start | bytes 4718596
  79.3 67.7 %reduce-scatter.4.cloned.1.call-start = ((), (), s32[]{:S(2)}) async-start(), calls=%async_computation.7 | async-start | bytes 1474560 | tf_op jit(solution)/shard_map/reduce_scatter | solution.py:79
  90.8 117.6 %all-gather.3.cloned.1.call-start = ((), (), s32[]{:S(2)}) async-start(), calls=%async_computation.9 | async-start | bytes 1474560 | tf_op jit(solution)/shard_map/all_gather | solution.py:91
  149.4 81.8 %all-gather.5.cloned.1.call-start = ((), (), s32[]{:S(2)}) async-start(), calls=%async_computation.11 | async-start | bytes 1474560 | tf_op jit(solution)/shard_map/all_gather | solution.py:93
  149.4 10.7 %collective-permute-start = (bf16[192,768]{1,0:T(8,128)(2,1)S(1)}, bf16[192,768]{1,0:T(8,128)(2,1)}, u32[]{:S(2)}, u32[]{:S(2)}) collective-permute-start(bf16[192,768]{1,0:T(8,128)(2,1)S(1)} %get-tuple-element.10), channel_id=1, source_target_pairs={{0,8},{8,16},{16,24},{24,0},{1,9},{9,17},{17,25},{25,1},{2,10},{10... | collective-permute-start | bytes 884744 | tf_op jit(solution)/shard_map/ppermute | solution.py:31
  160.1 17.5 %collective-permute-start.1 = (bf16[192,768]{1,0:T(8,128)(2,1)}, bf16[192,768]{1,0:T(8,128)(2,1)}, u32[]{:S(2)}, u32[]{:S(2)}) collective-permute-start(bf16[192,768]{1,0:T(8,128)(2,1)} %collective-permute-done), channel_id=1, source_target_pairs={{0,8},{8,16},{16,24},{24,0},{1,9},{9,17},{17,25},{25,1},{2,10},{10... | collective-permute-start | bytes 884744 | tf_op jit(solution)/shard_map/ppermute | solution.py:31
  177.7 14.4 %collective-permute-start.2 = (bf16[192,768]{1,0:T(8,128)(2,1)}, bf16[192,768]{1,0:T(8,128)(2,1)}, u32[]{:S(2)}, u32[]{:S(2)}) collective-permute-start(bf16[192,768]{1,0:T(8,128)(2,1)} %collective-permute-done.1), channel_id=1, source_target_pairs={{0,8},{8,16},{16,24},{24,0},{1,9},{9,17},{17,25},{25,1},{2,10},{10... | collective-permute-start | bytes 884744 | tf_op jit(solution)/shard_map/ppermute | solution.py:31
  226.7 31.9 %all-to-all-start.1 = ((bf16[8,96,1024]{2,1,0:T(8,128)(2,1)}), bf16[8,96,1024]{2,1,0:T(8,128)(2,1)}, u32[]{:S(2)}, u32[]{:S(2)}) async-start(bf16[8,96,1024]{2,1,0:T(8,128)(2,1)} %copy.76), calls=%async_computation.3 | async-start | bytes 3145728 | tf_op jit(solution)/shard_map/all_to_all | solution.py:116
  258.6 4.0 %copy-start.3 = (bf16[8,96,1024]{2,0,1:T(8,128)(2,1)S(1)}, bf16[8,96,1024]{2,0,1:T(8,128)(2,1)}, u32[]{:S(2)}) copy-start(bf16[8,96,1024]{2,0,1:T(8,128)(2,1)} %copy-done.2) | copy-start | bytes 4718596
  258.6 25.0 %all-to-all-start.3 = ((bf16[8,96,1024]{2,1,0:T(8,128)(2,1)}), bf16[8,96,1024]{2,1,0:T(8,128)(2,1)S(1)}, u32[]{:S(2)}, u32[]{:S(2)}) async-start(bf16[8,96,1024]{2,1,0:T(8,128)(2,1)} %copy.84), calls=%async_computation.6 | async-start | bytes 3145728 | tf_op jit(solution)/shard_map/all_to_all | solution.py:123
  262.6 8.1 %copy-start.4 = (s32[1024]{0:T(1024)S(1)}, s32[1024]{0:T(1024)}, u32[]{:S(2)}) copy-start(s32[1024]{0:T(1024)} %pad_clamp_fusion.1) | copy-start | bytes 12292
  283.6 2.1 copy-start.6
  283.6 2.1 copy-start.8
  283.6 4.4 %copy-start.1 = (bf16[48,1024]{1,0:T(8,128)(2,1)S(1)}, bf16[48,1024]{1,0:T(8,128)(2,1)}, u32[]{:S(2)}) copy-start(bf16[48,1024]{1,0:T(8,128)(2,1)} %param.10) | copy-start | bytes 294916
Sparse Core Ops, SparseCore 0:
  55.2 30.7 reduce-scatter.7
  88.9 27.8 reduce-scatter.5
  119.1 27.8 reduce-scatter.3
  149.5 39.1 all-gather.2
  190.2 29.6 all-gather.4
